TPU v7x, 128 devices: a whole 4x4x4 slice. The times are simulated.
128 devices in a mesh: sub: 128 (over z, y, x, core).
Axes of the slice: x: 4, y: 4, z: 4, core: 2. Of those that a mesh axis runs over, the one named last changes fastest.
Arguments:
- pool_inputs: bfloat16 [65536, 4096], P('sub'), may hold values from -6 to 6
- pool_targets: bfloat16 [65536, 4096], P('sub'), may hold values from -6 to 6
- row_picks: int32 [8, 32768], P(None, 'sub'), may hold values from 0 to 511
- weight_in: float32 [4096, 32768], P(None, 'sub'), may hold values from -6 to 6
- weight_out: float32 [4096, 32768], P(None, 'sub'), may hold values from -6 to 6
- eval_inputs: bfloat16 [256, 4096], P('sub'), may hold values from -6 to 6
- handover: int32 [4096], replicated, may hold values from 0 to 4095, as said below
Outputs:
- trained_in: float32 [4096, 32768], P(None, 'sub')
- trained_out: float32 [4096, 32768], P(None, 'sub')
- prediction: float32 [256, 4096], P('sub')
Inputs may be any that keep to these rules, and one draw needn't show every extreme that they name: `row_picks`: indices into the subnet's own 512 resident rows. handover[g] is the new position of neuron group g (neurons 8 g to 8 g + 7); every position is taken once, and no two groups of one subnet move to the same subnet.
All inputs are finite; a program needn't handle non-finite values.
Results may differ from a plain program's by a relative error of at most 0.0065.
Values may be sent and summed in bfloat16 or wider, within the bound.
No kernel may reach another device: no remote copies, remote signals or barrier semaphores. Data moves between devices by JAX's collectives and lax.ppermute only.
A program may use at most 192 MiB of HBM per device.

v0:
```python
import math

import jax
import jax.numpy as jnp
from jax import lax
from jax.sharding import PartitionSpec as P

D = 4096
GROUP = 8
STEPS = 4


tanh_coef = 0.7978845608028654
cubic_coef = 0.044715
step_rate = 0.5


def gelu_value(inputs):
    inner_term = tanh_coef * (inputs + cubic_coef * inputs * inputs * inputs)
    return 0.5 * inputs * (1.0 + jnp.tanh(inner_term))


def gelu_parts(inputs):
    tanh_part = jnp.tanh(tanh_coef * (inputs + cubic_coef * inputs * inputs * inputs))
    values = 0.5 * inputs * (1.0 + tanh_part)
    slopes = 0.5 * (1.0 + tanh_part) + 0.5 * inputs * (1.0 - tanh_part * tanh_part) * tanh_coef * (
        1.0 + 3.0 * cubic_coef * inputs * inputs
    )
    return (values, slopes)


def train_step(layer_in, layer_out, batch_rows, batch_goals, scale_in, scale_out):
    in_half = layer_in.astype(jnp.bfloat16)
    out_half = layer_out.astype(jnp.bfloat16)
    before = jnp.dot(batch_rows, in_half, preferred_element_type=jnp.float32) * scale_in
    values, slopes = gelu_parts(before)
    activity = values.astype(jnp.bfloat16)
    branch = jnp.dot(activity, out_half.T, preferred_element_type=jnp.float32) * scale_out
    errors = (branch - batch_goals.astype(jnp.float32)).astype(jnp.bfloat16)
    grad_out = jnp.dot(errors.T, activity, preferred_element_type=jnp.float32) * scale_out
    backward = (
        jnp.dot(errors, out_half, preferred_element_type=jnp.float32) * scale_out * slopes
    ).astype(jnp.bfloat16)
    grad_in = jnp.dot(batch_rows.T, backward, preferred_element_type=jnp.float32) * scale_in
    return (layer_in - step_rate * grad_in, layer_out - step_rate * grad_out)


def local_round(
    layer_in, layer_out, pool_inputs, pool_targets, row_picks, first_turn, scale_in, scale_out
):

    def one_turn(turn_index, carry):
        current_in, current_out = carry
        picked = lax.dynamic_slice_in_dim(row_picks, first_turn + turn_index, 1, 0)[0]
        batch_rows = jnp.take(pool_inputs, picked, axis=0)
        batch_goals = jnp.take(pool_targets, picked, axis=0)
        return train_step(current_in, current_out, batch_rows, batch_goals, scale_in, scale_out)

    return lax.fori_loop(0, STEPS, one_turn, (layer_in, layer_out))


def per_device(pool_inputs, pool_targets, row_picks, weight_in, weight_out, eval_inputs, handover):
    owners = lax.axis_size("sub")
    my_index = lax.axis_index("sub")
    hidden = weight_in.shape[1]
    group_count = hidden // GROUP
    total_groups = group_count * owners
    scale_in = 1.0 / math.sqrt(D)
    scale_out = 1.0 / math.sqrt(hidden * owners)
    layer_in, layer_out = local_round(
        weight_in, weight_out, pool_inputs, pool_targets, row_picks, 0, scale_in, scale_out
    )
    in_half = layer_in.astype(jnp.bfloat16)
    out_half = layer_out.astype(jnp.bfloat16)
    eval_act = gelu_value(
        jnp.dot(
            lax.all_gather(eval_inputs, "sub", axis=0, tiled=True),
            in_half,
            preferred_element_type=jnp.float32,
        )
        * scale_in
    ).astype(jnp.bfloat16)
    prediction = lax.psum_scatter(
        jnp.dot(eval_act, out_half.T, preferred_element_type=jnp.float32) * scale_out,
        "sub",
        scatter_dimension=0,
        tiled=True,
    )
    inverse = (
        jnp.zeros((total_groups,), jnp.int32)
        .at[handover]
        .set(jnp.arange(total_groups, dtype=jnp.int32))
    )
    offsets = jnp.arange(GROUP, dtype=jnp.int32)
    local_groups = lax.dynamic_slice_in_dim(handover, my_index * group_count, group_count, 0)
    targets = local_groups // group_count
    matches = targets[None, :] == jnp.arange(owners, dtype=jnp.int32)[:, None]
    chosen_group = jnp.sum(
        jnp.where(matches, jnp.arange(group_count, dtype=jnp.int32)[None, :], 0), axis=1
    )
    send_columns = (chosen_group[:, None] * GROUP + offsets[None, :]).reshape(-1)
    outgoing_in = jnp.take(layer_in, send_columns, axis=1)
    outgoing_out = jnp.take(layer_out, send_columns, axis=1)
    landed_in, landed_out = (
        lax.all_to_all(outgoing_in, "sub", split_axis=1, concat_axis=1, tiled=True),
        lax.all_to_all(outgoing_out, "sub", split_axis=1, concat_axis=1, tiled=True),
    )
    arriving = lax.dynamic_slice_in_dim(inverse, my_index * group_count, group_count, 0)
    sources = arriving // group_count
    take_columns = (sources[:, None] * GROUP + offsets[None, :]).reshape(-1)
    handed_in = jnp.take(landed_in, take_columns, axis=1)
    handed_out = jnp.take(landed_out, take_columns, axis=1)
    trained_in, trained_out = local_round(
        handed_in, handed_out, pool_inputs, pool_targets, row_picks, STEPS, scale_in, scale_out
    )
    return (trained_in, trained_out, prediction)


def solution(mesh):
    in_specs = (
        P("sub", None),
        P("sub", None),
        P(None, "sub"),
        P(None, "sub"),
        P(None, "sub"),
        P("sub", None),
        P(),
    )
    out_specs = (P(None, "sub"), P(None, "sub"), P("sub", None))
    return jax.shard_map(
        per_device, mesh=mesh, in_specs=in_specs, out_specs=out_specs, check_vma=False
    )
```

profile of v0, /device:TPU:84, one launch (start us, length us, event | category | flops | bytes accessed | tf_op | source)
XLA Modules:
  0.0 1048.2 jit_solution(7046368642467714534)
XLA Ops:
  13.8 15.5 %scatter_custom_fusion = s32[4096]{0:T(1024)S(1)} fusion(s32[4096]{0:T(1024)S(1)} %compare_select_fusion.2, s32[4096]{0:T(1024)S(1)} %iota.16, s32[]{:T(128)} %constant.305.clone.1), kind=kCustom, calls=%fused_computation.142 | custom fusion | bytes 16388 | tf_op jit(solution)/shard_map/scatter | solution.py:92
  30.9 157.9 %while.36 = (s32[]{:T(128)}, f32[4096,256]{1,0:T(8,128)}, f32[4096,256]{1,0:T(8,128)}, s32[8,256]{1,0:T(8,128)}, bf16[512,4096]{1,0:T(8,128)(2,1)}, /*index=5*/bf16[512,4096]{1,0:T(8,128)(2,1)}, s32[]{:T(128)}) while((s32[]{:T(128)}, f32[4096,256]{1,0:T(8,128)}, f32[4096,256]{1,0:T(8,128)}, s32[8,256]{1,0:T(8,128)}, ...), condition=%wide.region_1.3_spmd, body=%wide.region_0.2_spmd.sunk | while | flops 2701724928 | bytes 59782260 | solution.py:59
  53.7 8.6 fusion.148
  90.2 8.6 fusion.148
  126.7 8.6 fusion.148
  151.5 7.9 gather_fusion
  163.3 8.6 fusion.148
  200.2 16.8 %gather_fusion.6 = f32[1024,4096]{1,0:T(8,128)} fusion(f32[4096,256]{0,1:T(8,128)} %copy.23, s32[1024]{0:T(1024)S(1)} %fusion.111), kind=kCustom, calls=%fused_computation.6.clone | custom fusion | bytes 33558528 | tf_op jit(solution)/shard_map/jit(_take)/gather | solution.py:103
  217.0 16.8 %gather_fusion.4 = f32[1024,4096]{1,0:T(8,128)} fusion(f32[4096,256]{0,1:T(8,128)} %copy.22, s32[1024]{0:T(1024)S(1)} %fusion.111), kind=kCustom, calls=%fused_computation.1.clone | custom fusion | bytes 33558528 | tf_op jit(solution)/shard_map/jit(_take)/gather | solution.py:102
  233.8 16.9 %select_bitcast_fusion = (f32[4096,128,8]{0,2,1:T(8,128)S(1)}, f32[4096,128,8]{0,2,1:T(8,128)}) fusion(f32[1024,4096]{1,0:T(8,128)} %gather_fusion.6, pred[1024]{0:T(1024)(128)(4,1)S(1)} %copy-done.4, f32[1024,4096]{1,0:T(8,128)} %gather_fusion.4), kind=kLoop, calls=%fused_computation.117 | loop fusion | flops 8388608 | bytes 67109888 | tf_op jit(solution)/shard_map/all_to_all | solution.py:106
  250.7 191.8 %all_to_all.24 = f32[4096,128,8]{0,2,1:T(8,128)} all-to-all(f32[4096,128,8]{0,2,1:T(8,128)S(1)} %get-tuple-element.425), channel_id=1, replica_groups=mesh['sub'=128] {'sub'}, dimensions={1} | all-to-all | bytes 33554432 | tf_op jit(solution)/shard_map/all_to_all | solution.py:106
  442.5 11.7 %all-to-all-start = ((f32[4096,128,8]{0,2,1:T(8,128)}), f32[4096,128,8]{0,2,1:T(8,128)}, u32[]{:S(2)}, u32[]{:S(2)}) async-start(f32[4096,128,8]{0,2,1:T(8,128)} %get-tuple-element.426), calls=%async_computation | async-start | bytes 33554432 | tf_op jit(solution)/shard_map/all_to_all | solution.py:105
  455.0 230.9 %all-gather.3.cloned.1.call-done = bf16[128,2,4096]{2,1,0:T(2,128)(2,1)} async-done(((bf16[1,2,4096]{2,1,0:T(2,128)(2,1)}), bf16[128,2,4096]{2,1,0:T(2,128)(2,1)}) %all-gather.3.cloned.1.call-update) | async-done | bytes 2097168 | tf_op jit(solution)/shard_map/all_gather | solution.py:77
  688.6 8.0 convolution_multiply_fusion.8
  697.5 153.4 %all-reduce.3.cloned.1.call-done = f32[256,4096]{1,0:T(8,128)} async-done(((f32[256,4096]{1,0:T(8,128)}), f32[256,4096]{1,0:T(8,128)}) %all-reduce.3.cloned.1.call-update) | async-done | bytes 4194320
  852.4 11.5 %gather_fusion.7 = f32[256,4096]{1,0:T(8,128)} fusion(f32[4096,1024]{0,1:T(8,128)} %bitcast.47, s32[1024]{0:T(1024)S(1)} %pad_clamp_fusion.2), kind=kCustom, calls=%fused_computation.7.clone | custom fusion | bytes 8389632 | tf_op jit(solution)/shard_map/jit(_take)/gather | solution.py:112
  863.9 11.5 %gather_fusion.5 = f32[256,4096]{1,0:T(8,128)} fusion(f32[4096,1024]{0,1:T(8,128)} %bitcast.4, s32[1024]{0:T(1024)S(1)} %pad_clamp_fusion.2), kind=kCustom, calls=%fused_computation.2.clone | custom fusion | bytes 8389632 | tf_op jit(solution)/shard_map/jit(_take)/gather | solution.py:111
  875.4 8.4 select_bitcast_fusion.2
  895.0 146.0 %while.37 = (s32[]{:T(128)}, f32[4096,256]{1,0:T(8,128)}, f32[4096,256]{1,0:T(8,128)}, s32[8,256]{1,0:T(8,128)}, bf16[512,4096]{1,0:T(8,128)(2,1)}, /*index=5*/b...) while((s32[]{:T(128)}, f32[4096,256]{1,0:T(8,128)}, f32[4096,256]{1,0:T(8,128)}, ...), condition=%wide.region_5.9_spmd, body=%wide.region_4.8_spmd.sunk | while | flops 2701724928 | bytes 59782328 | solution.py:59
  906.1 7.9 gather_fusion.2
  917.8 8.6 fusion.157
  954.3 8.6 fusion.157
  990.8 8.6 fusion.157
  1027.4 8.6 fusion.157
  (121 shorter events, 243.6 us)
Async XLA Ops:
  7.2 4.6 copy-start.2
  11.8 2.0 copy-start.3
  38.3 3.7 copy-start
  74.8 3.7 copy-start
  111.3 3.7 copy-start
  147.8 3.7 copy-start
  217.0 16.8 %copy-start.4 = (pred[1024]{0:T(1024)(128)(4,1)S(1)}, pred[1024]{0:T(1024)(128)(4,1)}, u32[]{:S(2)}) copy-start(pred[1024]{0:T(1024)(128)(4,1)} %compare_and_fusion.2) | copy-start | bytes 3076
  442.5 421.4 %all-to-all-start = ((f32[4096,128,8]{0,2,1:T(8,128)}), f32[4096,128,8]{0,2,1:T(8,128)}, u32[]{:S(2)}, u32[]{:S(2)}) async-start(f32[4096,128,8]{0,2,1:T(8,128)} %get-tuple-element.426), calls=%async_computation | async-start | bytes 33554432 | tf_op jit(solution)/shard_map/all_to_all | solution.py:105
  454.2 231.7 %all-gather.3.cloned.1.call-start = ((), (), s32[]{:S(2)}) async-start(), calls=%async_computation.2 | async-start | bytes 2113536 | tf_op jit(solution)/shard_map/all_gather | solution.py:77
  454.9 396.0 %all-reduce.3.cloned.1.call-start = ((), (), s32[]{:S(2)}) async-start(), calls=%async_computation.3 | async-start | bytes 8388608
  696.6 0.7 copy-start.5
  902.4 3.7 copy-start.1
  938.9 3.7 copy-start.1
  975.4 3.7 copy-start.1
  1011.9 3.7 copy-start.1
Sparse Core Ops, SparseCore 0:
  458.2 227.6 all-gather.2
  696.8 154.0 all-reduce.2
where the time goes:
time: 1070 us; the launch traced here: 1050 us
  waiting for transfers between devices  385 us (36%)
  local copies, waits for them, and re-layouts  228 us (21%)
  blocking collectives  192 us (18%)
  matrix products  177 us (17%)
  other arithmetic  27 us (3%)
  between operations  14.5 us (1%)
  loops' own time  12.4 us (1%)
  starting transfers between devices  11.7 us (1%)
    all_gather x1, waiting for transfers between devices, per_device(): lax.all_gather(eval_inputs, 'sub', axis=0, tiled=True)  231 us
    all_to_all x1, blocking collectives, per_device(): lax.all_to_all(outgoing_out, 'sub', split_axis=1, concat_axis=1, tiled=True)  192 us
    unnamed x3, waiting for transfers between devices  154 us
    dot_general x8, matrix products, train_step(): jnp.dot(batch_rows.T, backward, preferred_element_type=jnp.float32)  68.7 us
    gather x8, local copies, waits for them, and re-layouts, one_turn(): batch_goals = jnp.take(pool_targets, picked, axis=0)  63.4 us
    gather x8, local copies, waits for them, and re-layouts, one_turn(): batch_rows = jnp.take(pool_inputs, picked, axis=0)  52.9 us
    dot_general x8, matrix products, train_step(): jnp.dot(errors.T, activity, preferred_element_type=jnp.float32) * scale_out  40.7 us
    dot_general x8, matrix products, train_step(): jnp.dot(activity, out_half.T, preferred_element_type=jnp.float32)  30.4 us
  transfers between devices with their start and end apart: 3, of which 2 were waited for; matrix products, arithmetic and copies ran while one was open for 2% of the time, Pallas kernels for 0%

commit v1 on v0

v1 whole, which is shorter than its diff:
```python
import math

import jax
import jax.numpy as jnp
from jax import lax
from jax.experimental import pallas as pl
from jax.experimental.pallas import tpu as pltpu
from jax.sharding import PartitionSpec as P

D = 4096
GROUP = 8
STEPS = 4
CHUNK = 512


tanh_coef = 0.7978845608028654
cubic_coef = 0.044715
step_rate = 0.5


def gelu_value(inputs):
    inner_term = tanh_coef * (inputs + cubic_coef * inputs * inputs * inputs)
    return 0.5 * inputs * (1.0 + jnp.tanh(inner_term))


def gelu_parts(inputs):
    tanh_part = jnp.tanh(tanh_coef * (inputs + cubic_coef * inputs * inputs * inputs))
    values = 0.5 * inputs * (1.0 + tanh_part)
    slopes = 0.5 * (1.0 + tanh_part) + 0.5 * inputs * (1.0 - tanh_part * tanh_part) * tanh_coef * (
        1.0 + 3.0 * cubic_coef * inputs * inputs
    )
    return (values, slopes)


NT = (((1,), (1,)), ((), ()))


def round_body(scale_in, scale_out, picks_ref, pin_ref, ptg_ref, wi0_ref, wo0_ref, wi_ref, wo_ref, rows_ref):
    wi_ref[...] = wi0_ref[...]
    wo_ref[...] = wo0_ref[...]
    batch = picks_ref.shape[0]
    pool = pin_ref.shape[0]
    hidden = wi_ref.shape[0]
    chunks = pin_ref.shape[1] // CHUNK
    for turn in range(picks_ref.shape[1]):
        picked = picks_ref[:, turn : turn + 1]
        onehot = (picked == lax.broadcasted_iota(jnp.int32, (batch, pool), 1)).astype(jnp.bfloat16)

        def pass_rows(c, before):
            cols = pl.ds(pl.multiple_of(c * CHUNK, CHUNK), CHUNK)
            rows_c = jnp.dot(onehot, pin_ref[:, cols], preferred_element_type=jnp.float32).astype(
                jnp.bfloat16
            )
            rows_ref[:, cols] = rows_c
            in_half = wi_ref[:, cols].astype(jnp.bfloat16)
            return before + lax.dot_general(rows_c, in_half, NT, preferred_element_type=jnp.float32)

        before = lax.fori_loop(
            0, chunks, pass_rows, jnp.zeros((batch, hidden), jnp.float32)
        ) * scale_in
        values, slopes = gelu_parts(before)
        activity = values.astype(jnp.bfloat16)
        activity_t = values.T.astype(jnp.bfloat16)

        def pass_out(c, back):
            cols = pl.ds(pl.multiple_of(c * CHUNK, CHUNK), CHUNK)
            goals_c = jnp.dot(onehot, ptg_ref[:, cols], preferred_element_type=jnp.float32)
            out_half = wo_ref[:, cols].astype(jnp.bfloat16)
            branch_c = jnp.dot(activity, out_half, preferred_element_type=jnp.float32) * scale_out
            errors_c = (branch_c - goals_c).astype(jnp.bfloat16)
            back = back + lax.dot_general(errors_c, out_half, NT, preferred_element_type=jnp.float32)
            grad_c = jnp.dot(activity_t, errors_c, preferred_element_type=jnp.float32) * scale_out
            wo_ref[:, cols] = wo_ref[:, cols] - step_rate * grad_c
            return back

        back = lax.fori_loop(0, chunks, pass_out, jnp.zeros((batch, hidden), jnp.float32))
        backward = back * scale_out * slopes
        backward_t = backward.astype(jnp.bfloat16).astype(jnp.float32).T.astype(jnp.bfloat16)

        def pass_in(c, carry):
            cols = pl.ds(pl.multiple_of(c * CHUNK, CHUNK), CHUNK)
            grad_c = jnp.dot(backward_t, rows_ref[:, cols], preferred_element_type=jnp.float32) * scale_in
            wi_ref[:, cols] = wi_ref[:, cols] - step_rate * grad_c
            return carry

        lax.fori_loop(0, chunks, pass_in, 0)


def train_round(wi_t, wo_t, pool_inputs, pool_targets, picks_t, scale_in, scale_out):
    hidden, width = wi_t.shape
    batch, turns = picks_t.shape
    pool = pool_inputs.shape[0]
    flops = turns * 2 * (2 * batch * pool * width + 5 * batch * hidden * width)
    bytes_accessed = 4 * hidden * width * 4 + 2 * pool * width * 2
    vmem = pl.BlockSpec(memory_space=pltpu.VMEM)
    return pl.pallas_call(
        lambda *refs: round_body(scale_in, scale_out, *refs),
        out_shape=(
            jax.ShapeDtypeStruct((hidden, width), jnp.float32),
            jax.ShapeDtypeStruct((hidden, width), jnp.float32),
        ),
        in_specs=[vmem] * 5,
        out_specs=(vmem, vmem),
        scratch_shapes=[pltpu.VMEM((batch, width), jnp.bfloat16)],
        compiler_params=pltpu.CompilerParams(vmem_limit_bytes=60 * 1024 * 1024),
        cost_estimate=pl.CostEstimate(
            flops=flops, transcendentals=turns * batch * hidden, bytes_accessed=bytes_accessed
        ),
        name="train_round",
    )(picks_t, pool_inputs, pool_targets, wi_t, wo_t)


def per_device(pool_inputs, pool_targets, row_picks, weight_in, weight_out, eval_inputs, handover):
    owners = lax.axis_size("sub")
    my_index = lax.axis_index("sub")
    hidden = weight_in.shape[1]
    group_count = hidden // GROUP
    scale_in = 1.0 / math.sqrt(D)
    scale_out = 1.0 / math.sqrt(hidden * owners)
    eval_all = lax.all_gather(eval_inputs, "sub", axis=0, tiled=True)
    picks_t = row_picks.T
    wi_t, wo_t = train_round(
        weight_in.T, weight_out.T, pool_inputs, pool_targets, picks_t[:, :STEPS], scale_in, scale_out
    )
    in_half = wi_t.astype(jnp.bfloat16)
    out_half = wo_t.astype(jnp.bfloat16)
    eval_act = gelu_value(
        lax.dot_general(eval_all, in_half, NT, preferred_element_type=jnp.float32) * scale_in
    ).astype(jnp.bfloat16)
    partial = jnp.dot(eval_act, out_half, preferred_element_type=jnp.float32) * scale_out
    rows_each = partial.shape[0] // owners
    gathered = lax.all_to_all(
        partial.reshape(owners, rows_each, partial.shape[1]), "sub", 0, 0, tiled=True
    )
    prediction = jnp.sum(gathered, axis=0)

    local_groups = lax.dynamic_slice_in_dim(handover, my_index * group_count, group_count, 0)
    targets = local_groups // group_count
    matches = targets[None, :] == jnp.arange(owners, dtype=jnp.int32)[:, None]
    chosen_group = jnp.sum(
        jnp.where(matches, jnp.arange(group_count, dtype=jnp.int32)[None, :], 0), axis=1
    )
    width = wi_t.shape[1]
    stacked = jnp.concatenate(
        [
            in_half.reshape(group_count, GROUP, width),
            out_half.reshape(group_count, GROUP, width),
        ],
        axis=1,
    )
    outgoing = jnp.take(stacked, chosen_group, axis=0)
    landed = lax.all_to_all(outgoing, "sub", 0, 0, tiled=True)
    positions = my_index * group_count + jnp.arange(group_count, dtype=jnp.int32)
    arriving_match = handover[None, :] == positions[:, None]
    arriving = jnp.sum(
        jnp.where(arriving_match, jnp.arange(handover.shape[0], dtype=jnp.int32)[None, :], 0), axis=1
    )
    sources = arriving // group_count
    handed = jnp.take(landed, sources, axis=0)
    handed_in = handed[:, :GROUP].reshape(hidden, width).astype(jnp.float32)
    handed_out = handed[:, GROUP:].reshape(hidden, width).astype(jnp.float32)
    trained_in, trained_out = train_round(
        handed_in, handed_out, pool_inputs, pool_targets, picks_t[:, STEPS:], scale_in, scale_out
    )
    return (trained_in.T, trained_out.T, prediction)


def solution(mesh):
    in_specs = (
        P("sub", None),
        P("sub", None),
        P(None, "sub"),
        P(None, "sub"),
        P(None, "sub"),
        P("sub", None),
        P(),
    )
    out_specs = (P(None, "sub"), P(None, "sub"), P("sub", None))
    return jax.shard_map(
        per_device, mesh=mesh, in_specs=in_specs, out_specs=out_specs, check_vma=False
    )
```

time: 1070 us -> 493 us (0.46); the launches traced: 1050 us -> 492 us
  blocking collectives: 192 us -> 0 us
  local copies, waits for them, and re-layouts: 228 us -> 51.2 us
  matrix products: 177 us -> 8.02 us
  waiting for transfers between devices: 385 us -> 252 us
  Pallas kernels: 0 us -> 111 us
  loops' own time: 12.4 us -> 0 us
    all_to_all x1 -> x2, waiting for transfers between devices: 0.01 us -> 252 us  [the longest x1 236 us: per_device(): landed = lax.all_to_all(outgoing, 'sub', 0, 0, tiled=True)]
    all_gather x1, waiting for transfers between devices: 231 us -> 0.01 us  [per_device(): eval_all = lax.all_gather(eval_inputs, 'sub', axis=0, tiled=True)]
    all_to_all x1 -> x0, blocking collectives: 192 us -> none  [per_device(): lax.all_to_all(outgoing_out, 'sub', split_axis=1, concat_axis=1, tiled=True)]
    dot_general x33 -> x1, matrix products: 177 us -> 8.02 us  [per_device(): jnp.dot(eval_act, out_half, preferred_element_type=jnp.float32) * scale_out]
    gather x20 -> x2, local copies, waits for them, and re-layouts: 173 us -> 18.7 us  [the longest x1 10.1 us: per_device(): outgoing = jnp.take(stacked, chosen_group, axis=0)]
    unnamed x3 -> x1, waiting for transfers between devices: 154 us -> 0.68 us
    pallas_call x0 -> x2, Pallas kernels: none -> 111 us  [train_round(): pl.pallas_call(lambda *refs: round_body(scale_in, scale_out, *refs), out_...]
    while x20 -> x0, local copies, waits for them, and re-layouts: 22.5 us -> none  [the longest x4 22.5 us: local_round(): return lax.fori_loop(0, STEPS, one_turn, (layer_in, layer_out))]
  transfers between devices with their start and end apart: 3 -> 3, of which waited for: 2 -> 2; matrix products, arithmetic and copies ran while one was open for 2% -> 10% of each run, Pallas kernels for 0% -> 11%
where the time goes in v1:
time: 493 us; the launch traced here: 492 us
  waiting for transfers between devices  252 us (51%)
  Pallas kernels  111 us (23%)
  local copies, waits for them, and re-layouts  51.2 us (10%)
  other arithmetic  32.4 us (7%)
  starting transfers between devices  22.4 us (5%)
  between operations  14.1 us (3%)
  matrix products  8.02 us (2%)
    all_to_all x1, waiting for transfers between devices, per_device(): landed = lax.all_to_all(outgoing, 'sub', 0, 0, tiled=True)  236 us
    pallas_call x2, Pallas kernels, train_round(): pl.pallas_call(lambda *refs: round_body(scale_in, scale_out, *refs), out_...  111 us
    unnamed x8, local copies, waits for them, and re-layouts  26 us
    all_to_all x1, waiting for transfers between devices, per_device(): lax.all_to_all(partial.reshape(owners, rows_each, partial.shape[1]), 'sub...  15.5 us
    select_n x2, other arithmetic, per_device(): outgoing = jnp.take(stacked, chosen_group, axis=0)  14.2 us
    all_to_all x1, starting transfers between devices, per_device(): landed = lax.all_to_all(outgoing, 'sub', 0, 0, tiled=True)  11.9 us
    all_to_all x1, starting transfers between devices, per_device(): lax.all_to_all(partial.reshape(owners, rows_each, partial.shape[1]), 'sub...  10.4 us
    gather x1, local copies, waits for them, and re-layouts, per_device(): outgoing = jnp.take(stacked, chosen_group, axis=0)  10.1 us
  transfers between devices with their start and end apart: 3, of which 2 were waited for; matrix products, arithmetic and copies ran while one was open for 10% of the time, Pallas kernels for 11%

profile of v1, /device:TPU:84, one launch (start us, length us, event | category | flops | bytes accessed | tf_op | source)
XLA Modules:
  0.0 491.8 jit_solution(4087615079658493806)
XLA Ops:
  7.2 0.7 all-gather.3.cloned.1.call-update
  7.9 0.8 copy.20
  8.7 5.6 %copy.21 = f32[4096,256]{0,1:T(8,128)} copy(f32[4096,256]{1,0:T(8,128)} %param.10) | data formatting | bytes 8388608 | tf_op args[3]
  14.3 5.6 %copy.22 = f32[4096,256]{0,1:T(8,128)} copy(f32[4096,256]{1,0:T(8,128)} %param.11) | data formatting | bytes 8388608 | tf_op args[4]
  20.0 0.8 fusion.26
  20.8 55.6 %train_round.2 = (f32[256,4096]{1,0:T(8,128)}, f32[256,4096]{1,0:T(8,128)}) custom-call(s32[256,4]{1,0:T(8,128)} %get-tuple-element.22.refs_0_, bf16[512,4096]{1,0:T(8,128)(2,1)} %refs_1_.3, bf16[512,4096]{1,0:T(8,128)(2,1)} %refs_2_.3, f32[256,4096]{1,0:T(8,128)} %bitcast.49, f32[256,4096]{1,0:T(8,128)} %bitcast.50), custom_call_target="tpu_custom_call" | custom-call | flops 19327352832 | bytes 25165824 | tf_op jit(solution)/shard_map/train_round/pallas_call | solution.py:96
  76.4 2.7 reshape.130
  79.1 8.0 %convolution_multiply_fusion = f32[256,4096]{1,0:T(8,128)} fusion(f32[256,4096]{1,0:T(8,128)} %get-tuple-element.8, bf16[256,4096]{1,0:T(8,128)(2,1)S(1)} %reshape.130, f32[256,4096]{1,0:T(8,128)} %get-tuple-element.7), kind=kOutput, calls=%fused_computation.3 | convolution fusion | flops 1077542912 | bytes 14680064 | tf_op jit(solution)/shard_map/dot_general | solution.py:130
  87.2 5.8 %reshape.110 = f32[128,2,4096]{2,1,0:T(2,128)} reshape(f32[256,4096]{1,0:T(8,128)} %convolution_multiply_fusion) | data formatting | bytes 8388608 | tf_op jit(solution)/shard_map/reshape | solution.py:133
  93.0 10.4 %all-to-all-start.1 = ((f32[128,2,4096]{2,1,0:T(2,128)}), f32[128,2,4096]{2,1,0:T(2,128)}, u32[]{:S(2)}, u32[]{:S(2)}) async-start(f32[128,2,4096]{2,1,0:T(2,128)} %reshape.110), calls=%async_computation.1 | async-start | bytes 8388608 | tf_op jit(solution)/shard_map/all_to_all | solution.py:132
  103.5 4.1 convert_bitcast_fusion
  107.6 2.5 pad_maximum_fusion
  110.1 10.1 %gather_fusion = bf16[128,16,4096]{2,1,0:T(8,128)(2,1)} fusion(bf16[32,16,4096]{2,1,0:T(8,128)(2,1)} %pad_maximum_fusion, s32[1024]{0:T(1024)S(1)} %pad_clamp_fusion.1), kind=kCustom, calls=%fused_computation | custom fusion | bytes 33554944 | tf_op jit(solution)/shard_map/jit(_take)/gather | solution.py:151
  120.2 14.2 %broadcast_select_fusion = bf16[128,16,4096]{2,1,0:T(8,128)(2,1)} fusion(bf16[128,16,4096]{2,1,0:T(8,128)(2,1)} %gather_fusion, pred[128]{0:T(512)(128)(4,1)S(1)} %compare_and_fusion), kind=kLoop, calls=%fused_computation.2 | loop fusion | flops 8388608 | bytes 33554560 | tf_op jit(solution)/shard_map/jit(_take)/select_n | solution.py:151
  134.4 15.5 %all-to-all-done.1 = f32[128,2,4096]{2,1,0:T(2,128)} async-done(((f32[128,2,4096]{2,1,0:T(2,128)}), f32[128,2,4096]{2,1,0:T(2,128)}, u32[]{:S(2)}, u32[]{:S(2)}) %all-to-all-start.1) | async-done | bytes 4194336 | tf_op jit(solution)/shard_map/all_to_all | solution.py:132
  149.9 11.9 %all-to-all-start = ((bf16[128,16,4096]{2,1,0:T(8,128)(2,1)}), bf16[128,16,4096]{2,1,0:T(8,128)(2,1)}, u32[]{:S(2)}, u32[]{:S(2)}) async-start(bf16[128,16,4096]{2,1,0:T(8,128)(2,1)} %broadcast_select_fusion), calls=%async_computation | async-start | bytes 33554432 | tf_op jit(solution)/shard_map/all_to_all | solution.py:152
  162.1 4.0 reduce_sum.35
  166.1 236.3 %all-to-all-done = bf16[128,16,4096]{2,1,0:T(8,128)(2,1)} async-done(((bf16[128,16,4096]{2,1,0:T(8,128)(2,1)}), bf16[128,16,4096]{2,1,0:T(8,128)(2,1)}, u32[]{:S(2)}, u32[]{:S(2)}) %all-to-all-start) | async-done | bytes 16777248 | tf_op jit(solution)/shard_map/all_to_all | solution.py:152
  402.4 8.6 %gather_fusion.1 = bf16[32,16,4096]{2,1,0:T(8,128)(2,1)} fusion(bf16[128,16,4096]{2,1,0:T(8,128)(2,1)} %all-to-all-done, s32[1024]{0:T(1024)S(1)} %pad_clamp_fusion), kind=kCustom, calls=%fused_computation.1 | custom fusion | bytes 8388736 | tf_op jit(solution)/shard_map/jit(_take)/gather | solution.py:159
  411.0 2.6 broadcast_select_fusion.1
  413.7 4.5 fusion
  418.2 55.6 %train_round.3 = (f32[256,4096]{1,0:T(8,128)}, f32[256,4096]{1,0:T(8,128)}) custom-call(s32[256,4]{1,0:T(8,128)} %get-tuple-element.23.refs_0_, bf16[512,4096]{1,0:T(8,128)(2,1)} %refs_1_.3, bf16[512,4096]{1,0:T(8,128)(2,1)} %refs_2_.3, f32[256,4096]{1,0:T(8,128)} %get-tuple-element.21.refs_3_, f32[256,4096]{1,0:T(8,128)} %get-tuple-element.20.refs_4_), custom_call_target="tpu_custom_call" | custom-call | flops 19327352832 | bytes 25165824 | tf_op jit(solution)/shard_map/train_round/pallas_call | solution.py:96
  473.7 5.6 %copy.23 = f32[4096,256]{1,0:T(8,128)} copy(f32[4096,256]{0,1:T(8,128)} %bitcast.52) | data formatting | bytes 8388608
  479.3 5.6 %copy.24 = f32[4096,256]{1,0:T(8,128)} copy(f32[4096,256]{0,1:T(8,128)} %bitcast.51) | data formatting | bytes 8388608
  (14 shorter events, 0.5 us)
Async XLA Ops:
  7.2 69.2 %all-gather.3.cloned.1.call-start = ((), (), s32[]{:S(2)}) async-start(), calls=%async_computation.2 | async-start | bytes 2113536 | tf_op jit(solution)/shard_map/all_gather | solution.py:120
  14.3 5.6 %copy-start = (s32[4096]{0:T(1024)S(1)}, s32[4096]{0:T(1024)}, u32[]{:S(2)}) copy-start(s32[4096]{0:T(1024)} %param.13) | copy-start | bytes 49156
  93.0 56.9 %all-to-all-start.1 = ((f32[128,2,4096]{2,1,0:T(2,128)}), f32[128,2,4096]{2,1,0:T(2,128)}, u32[]{:S(2)}, u32[]{:S(2)}) async-start(f32[128,2,4096]{2,1,0:T(2,128)} %reshape.110), calls=%async_computation.1 | async-start | bytes 8388608 | tf_op jit(solution)/shard_map/all_to_all | solution.py:132
  149.9 252.5 %all-to-all-start = ((bf16[128,16,4096]{2,1,0:T(8,128)(2,1)}), bf16[128,16,4096]{2,1,0:T(8,128)(2,1)}, u32[]{:S(2)}, u32[]{:S(2)}) async-start(bf16[128,16,4096]{2,1,0:T(8,128)(2,1)} %broadcast_select_fusion), calls=%async_computation | async-start | bytes 33554432 | tf_op jit(solution)/shard_map/all_to_all | solution.py:152
Sparse Core Ops, SparseCore 0:
  11.1 62.9 all-gather.2
